TPU v7x, 32 devices: a whole 2x2x4 slice. The times are simulated.
32 devices in a mesh: seq: 4 (over y, x), exp: 8 (over z, core).
Axes of the slice: x: 2, y: 2, z: 4, core: 2. Of those that a mesh axis runs over, the one named last changes fastest.
Arguments:
- token_ids: int32 [4, 32], replicated, may hold values from 0 to 51199
- cache_lengths: int32 [32], replicated, may hold values from 1 to 1024, as said below
- empty_blocks: int32 [32, 64], replicated, may hold values 0 or 1
- expert_ids: int32 [4, 32, 6], replicated, may hold values from 0 to 63, all different within a row
- embed_table: bfloat16 [51200, 2048], P(('seq', 'exp')), may hold values from -3 to 3
- attn_gain: float32 [2048], replicated, may hold values from 0.5 to 1.5
- w_query: bfloat16 [2048, 2048], P(None, 'seq'), may hold values from -0.125 to 0.125
- w_key: bfloat16 [2048, 2048], P(None, 'seq'), may hold values from -0.125 to 0.125
- w_value: bfloat16 [2048, 2048], P(None, 'seq'), may hold values from -0.125 to 0.125
- w_out: bfloat16 [2048, 2048], P('seq'), may hold values from -0.125 to 0.125
- k_cache: bfloat16 [32, 1024, 2048], P('exp', 'seq'), may hold values from -200 to 200
- v_cache: bfloat16 [32, 1024, 2048], P('exp', 'seq'), may hold values from -6 to 6
- moe_gain: float32 [2048], replicated, may hold values from 0.5 to 1.5
- w_router: bfloat16 [2048, 64], replicated, may hold values from -0.125 to 0.125
- gate_pieces: bfloat16 [256, 2048, 352], P(('seq', 'exp')), may hold values from -0.125 to 0.125
- up_pieces: bfloat16 [256, 2048, 352], P(('seq', 'exp')), may hold values from -0.125 to 0.125
- down_pieces: bfloat16 [256, 352, 2048], P(('seq', 'exp')), may hold values from -0.15625 to 0.15625
- shared_gate: bfloat16 [2048, 2816], P(None, 'exp'), may hold values from -0.125 to 0.125
- shared_up: bfloat16 [2048, 2816], P(None, 'exp'), may hold values from -0.125 to 0.125
- shared_down: bfloat16 [2816, 2048], P('exp'), may hold values from -0.109375 to 0.109375
- final_gain: float32 [2048], replicated, may hold values from 0.5 to 1.5
- w_head: bfloat16 [2048, 51200], P(None, ('seq', 'exp')), may hold values from -0.125 to 0.125
Outputs:
- hidden_norms: float32 [4, 32], replicated
- greatest_logits: float32 [4, 32], replicated
Inputs may be any that keep to these rules, and one draw needn't show every extreme that they name: `cache_lengths`: one of the 32 requests has exactly 1024 cached positions in every draw.
All inputs are finite; a program needn't handle non-finite values.
Results may differ from a plain program's by a relative error of at most 0.0055.
Values may be sent and summed in bfloat16 or wider, within the bound.
No kernel may reach another device: no remote copies, remote signals or barrier semaphores. Data moves between devices by JAX's collectives and lax.ppermute only.
A program may use at most 128 MiB of HBM per device.

v0:
```python
import math
import jax
import jax.numpy as jnp
from jax import lax
from jax.sharding import PartitionSpec as P

HDIM = 128
PIECES = 4
BLK = 16
epsilon = 1e-06
negative = -1e30


def rms_scale(values, scales):
    return values * lax.rsqrt(jnp.mean(values * values, axis=-1, keepdims=True) + epsilon) * scales


def rotate(values, places):
    half_width = values.shape[-1] // 2
    frequency = 10000.0 ** (-2.0 * jnp.arange(half_width, dtype=jnp.float32) / values.shape[-1])
    angles = places.astype(jnp.float32)[..., None, None] * frequency
    cosine_table = jnp.cos(angles)
    sine_table = jnp.sin(angles)
    lower = values[..., :half_width]
    upper = values[..., half_width:]
    return jnp.concatenate(
        [lower * cosine_table - upper * sine_table, upper * cosine_table + lower * sine_table],
        axis=-1,
    )


def gather_all(values):
    inner = lax.all_gather(values, "exp", axis=0, tiled=False)
    return lax.all_gather(inner, "seq", axis=0, tiled=False)


def on_device(
    token_ids,
    cache_lengths,
    empty_blocks,
    expert_ids,
    embed_table,
    attn_gain,
    w_query,
    w_key,
    w_value,
    w_out,
    k_cache,
    v_cache,
    moe_gain,
    w_router,
    gate_pieces,
    up_pieces,
    down_pieces,
    shared_gate,
    shared_up,
    shared_down,
    final_gain,
    w_head,
):
    steps, requests = token_ids.shape
    tokens = steps * requests
    width = embed_table.shape[1]
    vocab_local = embed_table.shape[0]
    n_seq = lax.axis_size("seq")
    n_exp = lax.axis_size("exp")
    n_dev = n_seq * n_exp
    owner_index = lax.axis_index(("seq", "exp"))
    seq_index = lax.axis_index("seq")
    own_count = requests // n_exp
    own_start = lax.axis_index("exp") * own_count
    group = steps * own_count
    share = group // n_seq

    def permuted(values):
        rest = values.shape[2:]
        grouped = jnp.moveaxis(values.reshape((steps, n_exp, own_count) + rest), 1, 0)
        split = grouped.reshape((n_exp, n_seq, share) + rest)
        return jnp.swapaxes(split, 0, 1).reshape((tokens,) + rest)

    def natural(values):
        split = jnp.swapaxes(values.reshape(n_seq, n_exp, share), 0, 1)
        grouped = split.reshape(n_exp, steps, own_count)
        return jnp.moveaxis(grouped, 0, 1).reshape(steps, requests)

    local_ids = token_ids - owner_index * vocab_local
    held = (local_ids >= 0) & (local_ids < vocab_local)
    rows = jnp.take(embed_table, jnp.clip(local_ids, 0, vocab_local - 1), axis=0)
    rows = jnp.where(held[..., None], rows, jnp.zeros((), rows.dtype))
    rows = jnp.moveaxis(rows.reshape(steps, n_exp, own_count, width), 1, 0)
    arrived = lax.all_to_all(rows, "exp", 0, 0, tiled=True)
    row_part = jnp.sum(arrived.astype(jnp.float32), axis=0).astype(jnp.bfloat16)
    row_parts = lax.all_gather(row_part, "seq", axis=0, tiled=False)
    embedded = jnp.sum(row_parts.astype(jnp.float32), axis=0).reshape(group, width)
    attn_in = rms_scale(embedded, attn_gain).astype(jnp.bfloat16)
    own_lengths = lax.dynamic_slice_in_dim(cache_lengths, own_start, own_count, 0)
    places = (own_lengths[None, :] + jnp.arange(steps, dtype=jnp.int32)[:, None]).reshape(group)
    heads_here = w_query.shape[1] // HDIM

    def project(weight):
        return jnp.dot(attn_in, weight, preferred_element_type=jnp.float32).reshape(
            group, heads_here, HDIM
        )

    query_part = rotate(project(w_query), places).astype(jnp.bfloat16)
    key_part = rotate(project(w_key), places).astype(jnp.bfloat16)
    value_part = project(w_value).astype(jnp.bfloat16)
    every = lax.all_gather(
        jnp.stack([query_part, key_part, value_part], axis=0), "seq", axis=0, tiled=False
    )
    head_count = n_seq * heads_here
    every = jnp.moveaxis(every, 0, 2).reshape(3, steps, own_count, head_count, HDIM)
    queries = every[0]
    span = k_cache.shape[1]
    first_place = seq_index * span
    places_here = first_place + jnp.arange(span, dtype=jnp.int32)
    own_empty = lax.dynamic_slice_in_dim(empty_blocks, own_start, own_count, 0)
    local_blocks = lax.dynamic_slice_in_dim(own_empty, first_place // BLK, span // BLK, 1)
    blocked = jnp.broadcast_to(local_blocks[:, :, None], (own_count, span // BLK, BLK)).reshape(
        own_count, span
    )
    live_mask = ((places_here[None, :] < own_lengths[:, None]) & (blocked == 0))[None, :, None, :]
    cache_keys = k_cache.reshape(own_count, span, head_count, HDIM)
    cache_values = v_cache.reshape(own_count, span, head_count, HDIM)
    score_scale = 1.0 / math.sqrt(HDIM)
    cached = (
        jnp.einsum("trhd,rphd->trhp", queries, cache_keys, preferred_element_type=jnp.float32)
        * score_scale
    )
    local_top = jnp.max(jnp.where(live_mask, cached, negative), axis=3)
    local_weights = jnp.where(live_mask, jnp.exp(cached - local_top[..., None]), 0.0)
    local_totals = jnp.sum(local_weights, axis=3)
    local_mixture = jnp.einsum(
        "trhp,rphd->trhd",
        local_weights.astype(jnp.bfloat16),
        cache_values,
        preferred_element_type=jnp.float32,
    )

    def by_owner(values):
        rest = values.shape[3:]
        split = values.reshape((steps, own_count, n_seq, heads_here) + rest)
        return jnp.moveaxis(split, 2, 0).reshape(n_seq, -1)

    mix_len = group * heads_here * HDIM
    stat_len = group * heads_here
    packed = jnp.concatenate(
        [by_owner(local_mixture), by_owner(local_top), by_owner(local_totals)], axis=1
    )
    got = lax.all_to_all(packed, "seq", 0, 0, tiled=True)
    got_mixture = got[:, :mix_len].reshape(n_seq, steps, own_count, heads_here, HDIM)
    got_top = got[:, mix_len : mix_len + stat_len].reshape(n_seq, steps, own_count, heads_here)
    got_totals = got[:, mix_len + stat_len :].reshape(n_seq, steps, own_count, heads_here)
    own_queries = query_part.reshape(steps, own_count, heads_here, HDIM)
    own_keys = key_part.reshape(steps, own_count, heads_here, HDIM)
    own_values = value_part.reshape(steps, own_count, heads_here, HDIM)
    fresh_scores = (
        jnp.einsum("trhd,urhd->trhu", own_queries, own_keys, preferred_element_type=jnp.float32)
        * score_scale
    )
    causal = (jnp.arange(steps)[None, :] <= jnp.arange(steps)[:, None])[:, None, None, :]
    fresh_top = jnp.max(jnp.where(causal, fresh_scores, negative), axis=3)
    fresh_weights = jnp.where(causal, jnp.exp(fresh_scores - fresh_top[..., None]), 0.0)
    fresh_mixture = jnp.einsum(
        "trhu,urhd->trhd",
        fresh_weights.astype(jnp.bfloat16),
        own_values,
        preferred_element_type=jnp.float32,
    )
    top_score = jnp.maximum(jnp.max(got_top, axis=0), fresh_top)
    cache_factor = jnp.exp(got_top - top_score[None])
    fresh_factor = jnp.exp(fresh_top - top_score)
    totals = (
        jnp.sum(got_totals * cache_factor, axis=0) + jnp.sum(fresh_weights, axis=3) * fresh_factor
    )
    mixture = (
        jnp.sum(got_mixture * cache_factor[..., None], axis=0)
        + fresh_mixture * fresh_factor[..., None]
    )
    own_heads = (mixture / totals[..., None]).astype(jnp.bfloat16).reshape(group, heads_here * HDIM)
    attn_part = jnp.dot(own_heads, w_out, preferred_element_type=jnp.float32)
    attn_sum = jnp.sum(
        lax.all_to_all(attn_part.reshape(n_seq, share, width), "seq", 0, 0, tiled=True), axis=0
    )
    resid_share = lax.dynamic_slice_in_dim(embedded, seq_index * share, share, 0) + attn_sum
    moe_in = gather_all(rms_scale(resid_share, moe_gain).astype(jnp.bfloat16)).reshape(
        tokens, width
    )
    router = jax.nn.sigmoid(jnp.dot(moe_in, w_router, preferred_element_type=jnp.float32))
    expert_count = w_router.shape[1]
    chosen_ids = permuted(expert_ids)
    picked = chosen_ids[:, :, None] == jnp.arange(expert_count, dtype=jnp.int32)[None, None, :]
    chosen = jnp.sum(jnp.where(picked, router[:, None, :], 0.0), axis=2)
    gate_weights = chosen / jnp.sum(chosen, axis=1, keepdims=True)
    rows_here = gate_pieces.shape[0]
    row_expert = (owner_index * rows_here + jnp.arange(rows_here, dtype=jnp.int32)) // PIECES
    token_weight = jnp.sum(
        jnp.where(
            chosen_ids[None, :, :] == row_expert[:, None, None], gate_weights[None, :, :], 0.0
        ),
        axis=2,
    )
    gate_out = jnp.einsum("nd,jdf->jnf", moe_in, gate_pieces, preferred_element_type=jnp.float32)
    up_out = jnp.einsum("nd,jdf->jnf", moe_in, up_pieces, preferred_element_type=jnp.float32)
    expert_hidden = (jax.nn.silu(gate_out) * up_out).astype(jnp.bfloat16)
    expert_out = jnp.einsum(
        "jnf,jfd->jnd", expert_hidden, down_pieces, preferred_element_type=jnp.float32
    )
    routed = jnp.einsum("jn,jnd->nd", token_weight, expert_out)
    share_count = tokens // n_seq
    share_start = seq_index * share_count
    share_rows = lax.dynamic_slice_in_dim(moe_in, share_start, share_count, 0)
    shared_hidden = (
        jax.nn.silu(jnp.dot(share_rows, shared_gate, preferred_element_type=jnp.float32))
        * jnp.dot(share_rows, shared_up, preferred_element_type=jnp.float32)
    ).astype(jnp.bfloat16)
    shared_out = jnp.dot(shared_hidden, shared_down, preferred_element_type=jnp.float32)
    term_rows = lax.dynamic_update_slice_in_dim(
        routed,
        lax.dynamic_slice_in_dim(routed, share_start, share_count, 0) + shared_out,
        share_start,
        0,
    )
    term_sum = jnp.sum(
        lax.all_to_all(term_rows.reshape(n_dev, share, width), ("seq", "exp"), 0, 0, tiled=True),
        axis=0,
    )
    final_share = resid_share + term_sum
    norms_share = jnp.sqrt(jnp.mean(final_share * final_share, axis=-1))
    head_in = gather_all(rms_scale(final_share, final_gain).astype(jnp.bfloat16)).reshape(
        tokens, width
    )
    local_best = jnp.max(jnp.dot(head_in, w_head, preferred_element_type=jnp.float32), axis=-1)
    message = jnp.concatenate([local_best, norms_share], axis=0)
    heard = lax.all_to_all(
        jnp.broadcast_to(message[None, :], (n_dev, message.shape[0])),
        ("seq", "exp"),
        0,
        0,
        tiled=True,
    )
    greatest_logits = natural(jnp.max(heard[:, :tokens], axis=0))
    hidden_norms = natural(heard[:, tokens:].reshape(tokens))
    return (hidden_norms, greatest_logits)


def solution(mesh):
    in_specs = (
        P(),
        P(),
        P(),
        P(),
        P(("seq", "exp"), None),
        P(),
        P(None, "seq"),
        P(None, "seq"),
        P(None, "seq"),
        P("seq", None),
        P("exp", "seq", None),
        P("exp", "seq", None),
        P(),
        P(),
        P(("seq", "exp"), None, None),
        P(("seq", "exp"), None, None),
        P(("seq", "exp"), None, None),
        P(None, "exp"),
        P(None, "exp"),
        P("exp", None),
        P(),
        P(None, ("seq", "exp")),
    )
    out_specs = (P(), P())
    return jax.shard_map(
        on_device, mesh=mesh, in_specs=in_specs, out_specs=out_specs, check_vma=False
    )
```

profile of v0, /device:TPU:0, one launch (start us, length us, event | category | flops | bytes accessed | tf_op | source)
XLA Modules:
  0.0 212.5 jit_solution(10068466699584656610)
XLA Ops:
  0.7 0.8 compare_and_fusion.1
  1.6 5.1 %gather_fusion = bf16[128,2048]{1,0:T(8,128)(2,1)S(1)} fusion(bf16[1600,2048]{1,0:T(8,128)(2,1)} %param.26, s32[1024]{0:T(1024)S(1)} %pad_clamp_fusion), kind=kCustom, calls=%fused_computation | custom fusion | bytes 1049088 | tf_op jit(solution)/shard_map/jit(_take)/gather | solution.py:88
  6.7 0.2 gather.7
  7.2 1.2 fusion.31
  8.4 6.3 %all-to-all-start = ((bf16[8,4,4,2048]{3,2,1,0:T(4,128)(2,1)}), bf16[8,4,4,2048]{3,2,1,0:T(4,128)(2,1)S(1)}, u32[]{:S(2)}, u32[]{:S(2)}) async-start(bf16[8,4,4,2048]{3,2,1,0:T(4,128)(2,1)} %fusion.31), calls=%async_computation | async-start | bytes 1048576 | tf_op jit(solution)/shard_map/all_to_all | solution.py:91
  14.8 4.0 %copy.152 = bf16[512,2048]{1,0:T(8,128)(2,1)} copy(bf16[512,2048]{0,1:T(8,128)(2,1)} %bitcast.138) | data formatting | bytes 4194304 | tf_op jit(solution)/shard_map/dot_general | solution.py:101
  18.8 3.9 %copy.153 = bf16[512,2048]{1,0:T(8,128)(2,1)} copy(bf16[512,2048]{0,1:T(8,128)(2,1)} %bitcast.139) | data formatting | bytes 4194304 | tf_op jit(solution)/shard_map/dot_general | solution.py:101
  22.8 4.0 %copy.154 = bf16[512,2048]{1,0:T(8,128)(2,1)} copy(bf16[512,2048]{0,1:T(8,128)(2,1)} %bitcast.140) | data formatting | bytes 4194304 | tf_op jit(solution)/shard_map/dot_general | solution.py:101
  26.8 0.8 dynamic-slice_compare_fusion
  28.1 2.0 all-to-all-done
  30.1 0.3 reduce_sum.137
  30.3 9.0 %all-gather = bf16[16,4,2048]{2,1,0:T(4,128)(2,1)S(1)} all-gather(bf16[4,4,2048]{2,1,0:T(4,128)(2,1)S(1)} %reduce_sum.137), channel_id=2, replica_groups=mesh['seq'=4,'exp'=8] {'seq'}, dimensions={0}, use_global_device_ids=true | all-gather | bytes 327680 | tf_op jit(solution)/shard_map/all_gather | solution.py:93
  39.7 2.4 %fusion.74 = f32[16,4,128]{2,0,1:T(8,128)S(1)} fusion(bf16[16,2048,1]{1,0,2:T(8,128)(2,1)S(1)} %reshape.564, bf16[4,128,2048]{2,1,0:T(8,128)(2,1)} %bitcast.136), kind=kOutput, calls=%fused_computation.132 | convolution fusion | flops 33554432 | bytes 2195456 | tf_op jit(solution)/shard_map/dot_general | solution.py:101
  42.1 0.7 fusion.75
  43.0 0.2 select_reduce_fusion.3
  43.4 2.2 %convolution_convert_fusion = bf16[16,4,128]{2,0,1:T(8,128)(2,1)S(1)} fusion(bf16[16,2048,1]{1,0,2:T(8,128)(2,1)S(1)} %reshape.564, bf16[4,128,2048]{2,1,0:T(8,128)(2,1)} %bitcast.134), kind=kOutput, calls=%fused_computation.34 | convolution fusion | flops 33562624 | bytes 2179072 | tf_op jit(solution)/shard_map/dot_general | solution.py:101
  45.7 8.8 %all-gather.1 = bf16[12,16,4,128]{3,1,2,0:T(8,128)(2,1)S(1)} all-gather(bf16[3,16,4,128]{3,1,2,0:T(8,128)(2,1)S(1)} %pad_maximum_fusion), channel_id=3, replica_groups=mesh['seq'=4,'exp'=8] {'seq'}, dimensions={0}, use_global_device_ids=true | all-gather | bytes 245760 | tf_op jit(solution)/shard_map/all_gather | solution.py:108
  54.7 3.5 %select_reduce_fusion = (f32[4,4,16]{0,2,1:T(8,128)S(1)}, f32[4,4,16,256]{3,0,2,1:T(4,128)S(1)}) fusion(pred[4,256]{1,0:T(4,128)(4,1)S(1)} %compare_and_fusion, bf16[4,4,16,128]{3,2,1,0:T(8,128)(2,1)S(1)} %bitcast.167, bf16[4,256,2048]{2,1,0:T(8,128)(2,1)} %param.32), kind=kOutput, calls=%fused_computation.42 | convolution fusion | flops 16973568 | bytes 4524032 | tf_op jit(solution)/shard_map/trhd,rphd->trhp/dot_general | solution.py:127
  58.2 0.3 fusion.32
  58.4 0.2 copy.134
  58.7 2.9 %fusion.2 = f32[4,16,4,128]{3,2,1,0:T(4,128)S(1)} fusion(f32[4,4,16,256]{3,0,2,1:T(4,128)S(1)} %get-tuple-element.27, f32[4,4,16]{0,2,1:T(8,128)S(1)} %get-tuple-element.26, pred[4,256]{1,0:T(4,128)(4,1)S(1)} %compare_and_fusion, bf16[4,256,2048]{2,1,0:T(8,128)(2,1)} %param.33), kind=kOutput, calls=%fused_computation.3 | convolution fusion | flops 16973824 | bytes 4589568 | tf_op jit(solution)/shard_map/trhp,rphd->trhd/dot_general | solution.py:133
  61.8 0.2 copy.132
  62.2 0.8 copy.135
  63.0 3.3 %all-to-all-start.1 = ((f32[4,1,8320]{2,1,0:T(1,128)}), f32[4,1,8320]{2,1,0:T(1,128)S(1)}, u32[]{:S(2)}, u32[]{:S(2)}) async-start(f32[4,1,8320]{2,1,0:T(1,128)} %copy.135), calls=%async_computation.1 | async-start | bytes 266240 | tf_op jit(solution)/shard_map/all_to_all | solution.py:150
  66.4 4.9 %all-to-all-done.1 = f32[4,1,8320]{2,1,0:T(1,128)S(1)} async-done(((f32[4,1,8320]{2,1,0:T(1,128)}), f32[4,1,8320]{2,1,0:T(1,128)S(1)}, u32[]{:S(2)}, u32[]{:S(2)}) %all-to-all-start.1) | async-done | bytes 133152 | tf_op jit(solution)/shard_map/all_to_all | solution.py:150
  72.5 0.2 fusion.28
  72.8 1.0 fusion.9
  73.8 3.5 %all-to-all-start.2 = ((f32[4,4,2048]{2,1,0:T(4,128)}), f32[4,4,2048]{2,1,0:T(4,128)S(1)}, u32[]{:S(2)}, u32[]{:S(2)}) async-start(f32[4,4,2048]{2,1,0:T(4,128)} %fusion.9), calls=%async_computation.2 | async-start | bytes 262144 | tf_op jit(solution)/shard_map/all_to_all | solution.py:183
  77.4 4.9 %all-to-all-done.2 = f32[4,4,2048]{2,1,0:T(4,128)S(1)} async-done(((f32[4,4,2048]{2,1,0:T(4,128)}), f32[4,4,2048]{2,1,0:T(4,128)S(1)}, u32[]{:S(2)}, u32[]{:S(2)}) %all-to-all-start.2) | async-done | bytes 131104 | tf_op jit(solution)/shard_map/all_to_all | solution.py:183
  82.5 14.0 %all-gather.6 = bf16[8,4,2048]{2,1,0:T(4,128)(2,1)S(1)} all-gather(bf16[1,4,2048]{2,1,0:T(4,128)(2,1)S(1)} %fusion.53), channel_id=4, replica_groups=mesh['seq'=4,'exp'=8] {'exp'}, dimensions={0}, use_global_device_ids=true | all-gather | bytes 147456 | tf_op jit(solution)/shard_map/all_gather | solution.py:33
  96.5 9.8 %all-gather.3 = bf16[32,4,2048]{2,1,0:T(4,128)(2,1)S(1)} all-gather(bf16[8,4,2048]{2,1,0:T(4,128)(2,1)S(1)} %all-gather.6), channel_id=5, replica_groups=mesh['seq'=4,'exp'=8] {'seq'}, dimensions={0}, use_global_device_ids=true | all-gather | bytes 655360 | tf_op jit(solution)/shard_map/all_gather | solution.py:34
  106.5 0.3 fusion.23
  107.1 6.2 %convolution_bitcast_fusion.1 = f32[8,128,352]{1,2,0:T(8,128)S(1)} fusion(bf16[128,2048,1]{1,0,2:T(8,128)(2,1)S(1)} %reshape.566, bf16[8,2048,352]{1,2,0:T(8,128)(2,1)} %param.36), kind=kOutput, calls=%fused_computation.14 | convolution fusion | flops 1476395008 | bytes 13500416 | tf_op jit(solution)/shard_map/nd,jdf->jnf/dot_general | solution.py:203
  113.4 18.6 %fusion.13 = bf16[8,128,2048]{2,1,0:T(8,128)(2,1)} fusion(bf16[8,352,2048]{2,1,0:T(8,128)(2,1)} %param.38, bf16[128,2048,1]{1,0,2:T(8,128)(2,1)S(1)} %reshape.566, bf16[8,2048,352]{1,2,0:T(8,128)(2,1)} %param.37, f32[8,128,352]{1,2,0:T(8,128)S(1)} %convolution_bitcast_fusion.1), kind=kOutput, calls=%fused_computation.17 | convolution fusion | flops 2954952704 | bytes 29229056 | tf_op jit(solution)/shard_map/jnf,jfd->jnd/dot_general | solution.py:206
  132.0 5.3 %fusion = f32[128,1,2048]{2,1,0:T(1,128)S(1)} fusion(bf16[8,128,1]{0,2,1:T(2,128)(2,1)S(1)} %copy.149, bf16[8,128,2048]{2,1,0:T(8,128)(2,1)} %fusion.13), kind=kOutput, calls=%fused_computation.1 | convolution fusion | flops 4194304 | bytes 5244928 | tf_op jit(solution)/shard_map/jn,jnd->nd/dot_general | solution.py:209
  137.3 0.3 copy.196
  137.7 1.0 copy-done.3
  138.7 0.5 fusion.41
  139.2 3.2 %fusion.8 = f32[128,2048]{1,0:T(8,128)S(1)} fusion(f32[128,2048]{1,0:T(8,128)S(1)} %bitcast.137, s32[]{:T(128)S(6)} %select_n.86, bf16[352,2048]{1,0:T(8,128)(2,1)} %param.41, bf16[2048,352]{0,1:T(8,128)(2,1)} %param.40, bf16[128,2048]{1,0:T(8,128)(2,1)S(1)} %reshape.535, f32[32,352]{1,0:T(8,128)S(1)} %fusion.41), kind=kOutput, calls=%fused_computation.10 | convolution fusion | flops 92407808 | bytes 3589120 | tf_op jit(solution)/shard_map/dot_general | solution.py:217
  142.4 0.3 reshape.536
  142.7 30.4 %all_to_all.36 = f32[32,4,2048]{2,1,0:T(4,128)S(1)} all-to-all(f32[32,4,2048]{2,1,0:T(4,128)S(1)} %reshape.536), channel_id=1, replica_groups=mesh['seq'=4,'exp'=8] {'seq','exp'}, dimensions={0} | all-to-all | bytes 2097152 | tf_op jit(solution)/shard_map/all_to_all | solution.py:225
  173.1 0.2 reduce_sum.151
  173.5 14.0 %all-gather.7 = bf16[8,4,2048]{2,1,0:T(4,128)(2,1)S(1)} all-gather(bf16[1,4,2048]{2,1,0:T(4,128)(2,1)S(1)} %fusion.54), channel_id=6, replica_groups=mesh['seq'=4,'exp'=8] {'exp'}, dimensions={0}, use_global_device_ids=true | all-gather | bytes 147456 | tf_op jit(solution)/shard_map/all_gather | solution.py:33
  187.4 9.4 %all-gather.5 = bf16[32,4,2048]{2,1,0:T(4,128)(2,1)S(1)} all-gather(bf16[8,4,2048]{2,1,0:T(4,128)(2,1)S(1)} %all-gather.7), channel_id=7, replica_groups=mesh['seq'=4,'exp'=8] {'seq'}, dimensions={0}, use_global_device_ids=true | all-gather | bytes 655360 | tf_op jit(solution)/shard_map/all_gather | solution.py:34
  196.9 4.9 %convolution_reduce_fusion = f32[128]{0:T(128)S(1)} fusion(bf16[128,2048]{1,0:T(8,128)(2,1)S(1)} %reshape.537, bf16[2048,1600]{0,1:T(8,128)(2,1)} %param.43), kind=kOutput, calls=%fused_computation.18 | convolution fusion | flops 839065472 | bytes 7078400 | tf_op jit(solution)/shard_map/dot_general | solution.py:233
  201.9 9.3 %all_to_all.37 = f32[32,1,132]{2,1,0:T(1,128)S(1)} all-to-all(f32[32,1,132]{2,1,0:T(1,128)S(1)} %broadcast_in_dim.150), channel_id=1, replica_groups=mesh['seq'=4,'exp'=8] {'seq','exp'}, dimensions={0} | all-to-all | bytes 33792 | tf_op jit(solution)/shard_map/all_to_all | solution.py:235
  211.2 0.7 reshape_reshape_reshape.3
  211.9 0.7 reshape_reshape.3
  (95 shorter events, 4.8 us)
Async XLA Ops:
  0.6 72.1 %copy-start = (bf16[512,2048]{1,0:T(8,128)(2,1)S(1)}, bf16[512,2048]{1,0:T(8,128)(2,1)}, u32[]{:S(2)}) copy-start(bf16[512,2048]{1,0:T(8,128)(2,1)} %param.31) | copy-start | bytes 6291460
  6.7 8.0 %copy-start.9 = (s32[32]{0:T(128)S(1)}, s32[32]{0:T(128)}, u32[]{:S(2)}) copy-start(s32[32]{0:T(128)} %param.23) | copy-start | bytes 388
  8.4 21.7 %all-to-all-start = ((bf16[8,4,4,2048]{3,2,1,0:T(4,128)(2,1)}), bf16[8,4,4,2048]{3,2,1,0:T(4,128)(2,1)S(1)}, u32[]{:S(2)}, u32[]{:S(2)}) async-start(bf16[8,4,4,2048]{3,2,1,0:T(4,128)(2,1)} %fusion.31), calls=%async_computation | async-start | bytes 1048576 | tf_op jit(solution)/shard_map/all_to_all | solution.py:91
  22.8 5.0 %copy-start.5 = (s32[4,32,6]{1,0,2:T(4,128)S(1)}, s32[4,32,6]{1,0,2:T(4,128)}, u32[]{:S(2)}) copy-start(s32[4,32,6]{1,0,2:T(4,128)} %param.25) | copy-start | bytes 9220
  22.8 16.8 %copy-start.6 = (f32[2048]{0:T(1024)S(1)}, f32[2048]{0:T(1024)}, u32[]{:S(2)}) copy-start(f32[2048]{0:T(1024)} %param.27) | copy-start | bytes 24580
  39.7 2.4 %copy-start.2 = (bf16[512,2048]{1,0:T(8,128)(2,1)S(1)}, bf16[512,2048]{1,0:T(8,128)(2,1)}, u32[]{:S(2)}) copy-start(bf16[512,2048]{1,0:T(8,128)(2,1)} %copy.153) | copy-start | bytes 6291460
  63.0 8.3 %all-to-all-start.1 = ((f32[4,1,8320]{2,1,0:T(1,128)}), f32[4,1,8320]{2,1,0:T(1,128)S(1)}, u32[]{:S(2)}, u32[]{:S(2)}) async-start(f32[4,1,8320]{2,1,0:T(1,128)} %copy.135), calls=%async_computation.1 | async-start | bytes 266240 | tf_op jit(solution)/shard_map/all_to_all | solution.py:150
  72.3 10.1 %copy-start.7 = (f32[2048]{0:T(1024)S(1)}, f32[2048]{0:T(1024)}, u32[]{:S(2)}) copy-start(f32[2048]{0:T(1024)} %param.34) | copy-start | bytes 24580
  73.8 32.7 %copy-start.4 = (bf16[2048,64]{0,1:T(8,128)(2,1)S(1)}, bf16[2048,64]{0,1:T(8,128)(2,1)}, u32[]{:S(2)}) copy-start(bf16[2048,64]{0,1:T(8,128)(2,1)} %param.35) | copy-start | bytes 786436
  73.8 8.4 %all-to-all-start.2 = ((f32[4,4,2048]{2,1,0:T(4,128)}), f32[4,4,2048]{2,1,0:T(4,128)S(1)}, u32[]{:S(2)}, u32[]{:S(2)}) async-start(f32[4,4,2048]{2,1,0:T(4,128)} %fusion.9), calls=%async_computation.2 | async-start | bytes 262144 | tf_op jit(solution)/shard_map/all_to_all | solution.py:183
  137.3 1.4 copy-start.3
  142.7 30.7 %copy-start.8 = (f32[2048]{0:T(1024)S(1)}, f32[2048]{0:T(1024)}, u32[]{:S(2)}) copy-start(f32[2048]{0:T(1024)} %param.42) | copy-start | bytes 24580
  196.9 15.6 %copy-start.1 = (bf16[512,2048]{1,0:T(8,128)(2,1)S(1)}, bf16[512,2048]{1,0:T(8,128)(2,1)}, u32[]{:S(2)}) copy-start(bf16[512,2048]{1,0:T(8,128)(2,1)} %param.31) | copy-start | bytes 6291460
where the time goes:
time: 214 us; the launch traced here: 213 us
  blocking collectives  105 us (49%)
  matrix products  52.2 us (24%)
  local copies, waits for them, and re-layouts  24.4 us (11%)
  starting transfers between devices  13.1 us (6%)
  waiting for transfers between devices  11.9 us (6%)
  other arithmetic  5.27 us (2%)
    all_to_all x1, blocking collectives, on_device(): lax.all_to_all(term_rows.reshape(n_dev, share, width), ('seq', 'exp'), 0,...  30.4 us
    all_gather x2, blocking collectives, gather_all(): inner = lax.all_gather(values, 'exp', axis=0, tiled=False)  27.9 us
    all_gather x2, blocking collectives, gather_all(): return lax.all_gather(inner, 'seq', axis=0, tiled=False)  19.1 us
    dot_general x1, matrix products, on_device(): jnp.einsum('jnf,jfd->jnd', expert_hidden, down_pieces, preferred_element_...  18.6 us
    dot_general x3, local copies, waits for them, and re-layouts, project(): jnp.dot(attn_in, weight, preferred_element_type=jnp.float32)  11.9 us
    all_to_all x1, blocking collectives, on_device(): lax.all_to_all(jnp.broadcast_to(message[None, :], (n_dev, message.shape[0...  9.33 us
    all_gather x1, blocking collectives, on_device(): row_parts = lax.all_gather(row_part, 'seq', axis=0, tiled=False)  9 us
    all_gather x1, blocking collectives, on_device(): lax.all_gather(jnp.stack([query_part, key_part, value_part], axis=0), 'se...  8.83 us
  transfers between devices with their start and end apart: 3, of which 3 were waited for; matrix products, arithmetic and copies ran while one was open for 6% of the time, Pallas kernels for 0%

commit v1 on v0

--- a/solution.py
+++ b/solution.py
@@ -9,6 +9,17 @@
 BLK = 16
 epsilon = 1e-06
 negative = -1e30
+
+
+def split_up(array, dim, size):
+    before, after = (array.shape[:dim], array.shape[dim + 1 :])
+    return jnp.moveaxis(array.reshape(*before, size, -1, *after), dim, 0)
+
+
+def joined_along(tiles, dim):
+    shape = list(tiles.shape[1:])
+    shape[dim] *= tiles.shape[0]
+    return jnp.moveaxis(tiles, 0, dim).reshape(shape)
 
 
 def rms_scale(values, scales):
@@ -147,7 +158,14 @@
     packed = jnp.concatenate(
         [by_owner(local_mixture), by_owner(local_top), by_owner(local_totals)], axis=1
     )
-    got = lax.all_to_all(packed, "seq", 0, 0, tiled=True)
+    length, index = (lax.axis_size("seq"), lax.axis_index("seq"))
+    tiles = split_up(packed, 0, length)
+    gathered = [tiles[index]]
+    for step in range(1, length):
+        sent = tiles[index ^ step]
+        gathered.append(lax.ppermute(sent, "seq", [(i, i ^ step) for i in range(length)]))
+    tiles = jnp.stack(gathered)[index ^ jnp.arange(length)]
+    got = joined_along(tiles, 0)
     got_mixture = got[:, :mix_len].reshape(n_seq, steps, own_count, heads_here, HDIM)
     got_top = got[:, mix_len : mix_len + stat_len].reshape(n_seq, steps, own_count, heads_here)
     got_totals = got[:, mix_len + stat_len :].reshape(n_seq, steps, own_count, heads_here)

time: 214 us -> 210 us (0.981)
  waiting for transfers between devices: 11.9 us -> 9.75 us
    all_to_all x1 -> x0, waiting for transfers between devices: 4.95 us -> none  [on_device(): got = lax.all_to_all(packed, 'seq', 0, 0, tiled=True)]
    ppermute x0 -> x3, starting transfers between devices: none -> 3.55 us  [on_device(): lax.ppermute(sent, 'seq', [(i, i ^ step) for i in range(length)])]
    all_to_all x1 -> x0, starting transfers between devices: 3.32 us -> none  [on_device(): got = lax.all_to_all(packed, 'seq', 0, 0, tiled=True)]
    ppermute x0 -> x3, waiting for transfers between devices: none -> 2.86 us  [on_device(): lax.ppermute(sent, 'seq', [(i, i ^ step) for i in range(length)])]
  transfers between devices with their start and end apart: 3 -> 5, of which waited for: 3 -> 4; matrix products, arithmetic and copies ran while one was open for 6% -> 7% of each run, Pallas kernels for 0% -> 0%
where the time goes in v1:
time: 210 us; the launch traced here: 209 us
  blocking collectives  105 us (50%)
  matrix products  50.6 us (24%)
  local copies, waits for them, and re-layouts  24.3 us (12%)
  starting transfers between devices  13.3 us (6%)
  waiting for transfers between devices  9.75 us (5%)
  other arithmetic  5.42 us (3%)
    all_to_all x1, blocking collectives, on_device(): lax.all_to_all(term_rows.reshape(n_dev, share, width), ('seq', 'exp'), 0,...  30.4 us
    all_gather x2, blocking collectives, gather_all(): inner = lax.all_gather(values, 'exp', axis=0, tiled=False)  27.9 us
    all_gather x2, blocking collectives, gather_all(): return lax.all_gather(inner, 'seq', axis=0, tiled=False)  19.1 us
    dot_general x1, matrix products, on_device(): jnp.einsum('jnf,jfd->jnd', expert_hidden, down_pieces, preferred_element_...  18.6 us
    dot_general x3, local copies, waits for them, and re-layouts, project(): jnp.dot(attn_in, weight, preferred_element_type=jnp.float32)  11.9 us
    all_to_all x1, blocking collectives, on_device(): lax.all_to_all(jnp.broadcast_to(message[None, :], (n_dev, message.shape[0...  9.33 us
    all_gather x1, blocking collectives, on_device(): row_parts = lax.all_gather(row_part, 'seq', axis=0, tiled=False)  9 us
    all_gather x1, blocking collectives, on_device(): lax.all_gather(jnp.stack([query_part, key_part, value_part], axis=0), 'se...  8.83 us
  transfers between devices with their start and end apart: 5, of which 4 were waited for; matrix products, arithmetic and copies ran while one was open for 7% of the time, Pallas kernels for 0%

profile of v1, /device:TPU:0, one launch (start us, length us, event | category | flops | bytes accessed | tf_op | source)
XLA Modules:
  0.0 209.2 jit_solution(15471977043995112771)
XLA Ops:
  0.7 0.8 compare_and_fusion.1
  1.6 5.1 %gather_fusion = bf16[128,2048]{1,0:T(8,128)(2,1)S(1)} fusion(bf16[1600,2048]{1,0:T(8,128)(2,1)} %param.26, s32[1024]{0:T(1024)S(1)} %pad_clamp_fusion.1), kind=kCustom, calls=%fused_computation | custom fusion | bytes 1049088 | tf_op jit(solution)/shard_map/jit(_take)/gather | solution.py:99
  7.2 1.2 fusion.31
  8.4 6.3 %all-to-all-start = ((bf16[8,4,4,2048]{3,2,1,0:T(4,128)(2,1)}), bf16[8,4,4,2048]{3,2,1,0:T(4,128)(2,1)S(1)}, u32[]{:S(2)}, u32[]{:S(2)}) async-start(bf16[8,4,4,2048]{3,2,1,0:T(4,128)(2,1)} %fusion.31), calls=%async_computation | async-start | bytes 1048576 | tf_op jit(solution)/shard_map/all_to_all | solution.py:102
  14.8 0.8 dynamic-slice_compare_fusion
  15.6 4.0 %copy.150 = bf16[512,2048]{1,0:T(8,128)(2,1)} copy(bf16[512,2048]{0,1:T(8,128)(2,1)} %bitcast.143) | data formatting | bytes 4194304 | tf_op jit(solution)/shard_map/dot_general | solution.py:112
  19.6 3.9 %copy.151 = bf16[512,2048]{1,0:T(8,128)(2,1)} copy(bf16[512,2048]{0,1:T(8,128)(2,1)} %bitcast.144) | data formatting | bytes 4194304 | tf_op jit(solution)/shard_map/dot_general | solution.py:112
  23.6 4.0 %copy.152 = bf16[512,2048]{1,0:T(8,128)(2,1)} copy(bf16[512,2048]{0,1:T(8,128)(2,1)} %bitcast.145) | data formatting | bytes 4194304 | tf_op jit(solution)/shard_map/dot_general | solution.py:112
  28.1 2.0 all-to-all-done
  30.1 0.3 reduce_sum.137
  30.3 9.0 %all-gather = bf16[16,4,2048]{2,1,0:T(4,128)(2,1)S(1)} all-gather(bf16[4,4,2048]{2,1,0:T(4,128)(2,1)S(1)} %reduce_sum.137), channel_id=2, replica_groups=mesh['seq'=4,'exp'=8] {'seq'}, dimensions={0}, use_global_device_ids=true | all-gather | bytes 327680 | tf_op jit(solution)/shard_map/all_gather | solution.py:104
  39.7 2.4 %fusion.75 = f32[16,4,128]{2,0,1:T(8,128)S(1)} fusion(bf16[16,2048,1]{1,0,2:T(8,128)(2,1)S(1)} %reshape.601, bf16[4,128,2048]{2,1,0:T(8,128)(2,1)} %bitcast.141), kind=kOutput, calls=%fused_computation.140 | convolution fusion | flops 33554432 | bytes 2195456 | tf_op jit(solution)/shard_map/dot_general | solution.py:112
  42.1 0.7 fusion.76
  43.0 0.6 convolution_convert_fusion
  43.7 8.8 %all-gather.1 = bf16[12,16,4,128]{3,1,2,0:T(8,128)(2,1)S(1)} all-gather(bf16[3,16,4,128]{3,1,2,0:T(8,128)(2,1)S(1)} %pad_maximum_fusion), channel_id=3, replica_groups=mesh['seq'=4,'exp'=8] {'seq'}, dimensions={0}, use_global_device_ids=true | all-gather | bytes 245760 | tf_op jit(solution)/shard_map/all_gather | solution.py:119
  52.7 3.5 %select_reduce_fusion = (f32[4,4,16]{0,2,1:T(8,128)S(1)}, f32[4,4,16,256]{3,0,2,1:T(4,128)S(1)}) fusion(pred[4,256]{1,0:T(4,128)(4,1)S(1)} %compare_and_fusion, bf16[4,4,16,128]{3,2,1,0:T(8,128)(2,1)S(1)} %bitcast.168, bf16[4,256,2048]{2,1,0:T(8,128)(2,1)} %param.32), kind=kOutput, calls=%fused_computation.43 | convolution fusion | flops 16973568 | bytes 4524032 | tf_op jit(solution)/shard_map/trhd,rphd->trhp/dot_general | solution.py:138
  56.1 0.3 fusion.32
  56.4 0.2 copy.133
  56.7 2.9 %fusion.2 = f32[4,16,4,128]{3,2,1,0:T(4,128)S(1)} fusion(f32[4,4,16,256]{3,0,2,1:T(4,128)S(1)} %get-tuple-element.31, f32[4,4,16]{0,2,1:T(8,128)S(1)} %get-tuple-element.30, pred[4,256]{1,0:T(4,128)(4,1)S(1)} %compare_and_fusion, bf16[4,256,2048]{2,1,0:T(8,128)(2,1)} %param.33), kind=kOutput, calls=%fused_computation.4 | convolution fusion | flops 16973824 | bytes 4589568 | tf_op jit(solution)/shard_map/trhp,rphd->trhd/dot_general | solution.py:144
  60.3 0.5 collective-permute-start
  60.8 1.6 collective-permute-start.1
  62.4 1.5 collective-permute-start.2
  63.9 0.2 select_reduce_fusion.3
  64.4 0.3 collective-permute-done.1
  64.7 2.5 %collective-permute-done.2 = f32[1,8320]{1,0:T(1,128)S(1)} collective-permute-done((f32[1,8320]{1,0:T(1,128)S(1)}, f32[1,8320]{1,0:T(1,128)S(1)}, u32[]{:S(2)}, u32[]{:S(2)}) %collective-permute-start.2) | collective-permute-done | bytes 33312 | tf_op jit(solution)/shard_map/ppermute | solution.py:166
  67.4 0.6 gather_fusion.1
  69.1 0.2 fusion.28
  69.4 1.0 fusion.9
  70.5 3.5 %all-to-all-start.1 = ((f32[4,4,2048]{2,1,0:T(4,128)}), f32[4,4,2048]{2,1,0:T(4,128)S(1)}, u32[]{:S(2)}, u32[]{:S(2)}) async-start(f32[4,4,2048]{2,1,0:T(4,128)} %fusion.9), calls=%async_computation.1 | async-start | bytes 262144 | tf_op jit(solution)/shard_map/all_to_all | solution.py:201
  74.0 4.9 %all-to-all-done.1 = f32[4,4,2048]{2,1,0:T(4,128)S(1)} async-done(((f32[4,4,2048]{2,1,0:T(4,128)}), f32[4,4,2048]{2,1,0:T(4,128)S(1)}, u32[]{:S(2)}, u32[]{:S(2)}) %all-to-all-start.1) | async-done | bytes 131104 | tf_op jit(solution)/shard_map/all_to_all | solution.py:201
  79.2 14.0 %all-gather.6 = bf16[8,4,2048]{2,1,0:T(4,128)(2,1)S(1)} all-gather(bf16[1,4,2048]{2,1,0:T(4,128)(2,1)S(1)} %fusion.53), channel_id=4, replica_groups=mesh['seq'=4,'exp'=8] {'exp'}, dimensions={0}, use_global_device_ids=true | all-gather | bytes 147456 | tf_op jit(solution)/shard_map/all_gather | solution.py:44
  93.1 9.8 %all-gather.3 = bf16[32,4,2048]{2,1,0:T(4,128)(2,1)S(1)} all-gather(bf16[8,4,2048]{2,1,0:T(4,128)(2,1)S(1)} %all-gather.6), channel_id=5, replica_groups=mesh['seq'=4,'exp'=8] {'seq'}, dimensions={0}, use_global_device_ids=true | all-gather | bytes 655360 | tf_op jit(solution)/shard_map/all_gather | solution.py:45
  103.2 0.3 fusion.23
  103.8 6.2 %convolution_bitcast_fusion.1 = f32[8,128,352]{1,2,0:T(8,128)S(1)} fusion(bf16[128,2048,1]{1,0,2:T(8,128)(2,1)S(1)} %reshape.603, bf16[8,2048,352]{1,2,0:T(8,128)(2,1)} %param.36), kind=kOutput, calls=%fused_computation.15 | convolution fusion | flops 1476395008 | bytes 13500416 | tf_op jit(solution)/shard_map/nd,jdf->jnf/dot_general | solution.py:221
  110.0 18.6 %fusion.13 = bf16[8,128,2048]{2,1,0:T(8,128)(2,1)} fusion(bf16[8,352,2048]{2,1,0:T(8,128)(2,1)} %param.38, bf16[128,2048,1]{1,0,2:T(8,128)(2,1)S(1)} %reshape.603, bf16[8,2048,352]{1,2,0:T(8,128)(2,1)} %param.37, f32[8,128,352]{1,2,0:T(8,128)S(1)} %convolution_bitcast_fusion.1), kind=kOutput, calls=%fused_computation.18 | convolution fusion | flops 2954952704 | bytes 29229056 | tf_op jit(solution)/shard_map/jnf,jfd->jnd/dot_general | solution.py:224
  128.6 5.3 %fusion = f32[128,1,2048]{2,1,0:T(1,128)S(1)} fusion(bf16[8,128,1]{0,2,1:T(2,128)(2,1)S(1)} %copy.147, bf16[8,128,2048]{2,1,0:T(8,128)(2,1)} %fusion.13), kind=kOutput, calls=%fused_computation.2 | convolution fusion | flops 4194304 | bytes 5244928 | tf_op jit(solution)/shard_map/jn,jnd->nd/dot_general | solution.py:227
  134.0 0.3 copy.192
  134.3 1.0 copy-done.4
  135.3 0.5 fusion.41
  135.8 3.2 %fusion.8 = f32[128,2048]{1,0:T(8,128)S(1)} fusion(f32[128,2048]{1,0:T(8,128)S(1)} %bitcast.142, s32[]{:T(128)S(6)} %select_n.113, bf16[352,2048]{1,0:T(8,128)(2,1)} %param.41, bf16[2048,352]{0,1:T(8,128)(2,1)} %param.40, bf16[128,2048]{1,0:T(8,128)(2,1)S(1)} %reshape.561, f32[32,352]{1,0:T(8,128)S(1)} %fusion.41), kind=kOutput, calls=%fused_computation.11 | convolution fusion | flops 92407808 | bytes 3589120 | tf_op jit(solution)/shard_map/dot_general | solution.py:235
  139.0 0.3 reshape.562
  139.3 30.4 %all_to_all.24 = f32[32,4,2048]{2,1,0:T(4,128)S(1)} all-to-all(f32[32,4,2048]{2,1,0:T(4,128)S(1)} %reshape.562), channel_id=1, replica_groups=mesh['seq'=4,'exp'=8] {'seq','exp'}, dimensions={0} | all-to-all | bytes 2097152 | tf_op jit(solution)/shard_map/all_to_all | solution.py:243
  170.1 14.0 %all-gather.7 = bf16[8,4,2048]{2,1,0:T(4,128)(2,1)S(1)} all-gather(bf16[1,4,2048]{2,1,0:T(4,128)(2,1)S(1)} %fusion.54), channel_id=6, replica_groups=mesh['seq'=4,'exp'=8] {'exp'}, dimensions={0}, use_global_device_ids=true | all-gather | bytes 147456 | tf_op jit(solution)/shard_map/all_gather | solution.py:44
  184.1 9.4 %all-gather.5 = bf16[32,4,2048]{2,1,0:T(4,128)(2,1)S(1)} all-gather(bf16[8,4,2048]{2,1,0:T(4,128)(2,1)S(1)} %all-gather.7), channel_id=7, replica_groups=mesh['seq'=4,'exp'=8] {'seq'}, dimensions={0}, use_global_device_ids=true | all-gather | bytes 655360 | tf_op jit(solution)/shard_map/all_gather | solution.py:45
  193.6 4.9 %convolution_reduce_fusion = f32[128]{0:T(128)S(1)} fusion(bf16[128,2048]{1,0:T(8,128)(2,1)S(1)} %reshape.563, bf16[2048,1600]{0,1:T(8,128)(2,1)} %param.43), kind=kOutput, calls=%fused_computation.19 | convolution fusion | flops 839065472 | bytes 7078400 | tf_op jit(solution)/shard_map/dot_general | solution.py:251
  198.5 9.3 %all_to_all.25 = f32[32,1,132]{2,1,0:T(1,128)S(1)} all-to-all(f32[32,1,132]{2,1,0:T(1,128)S(1)} %broadcast_in_dim.151), channel_id=1, replica_groups=mesh['seq'=4,'exp'=8] {'seq','exp'}, dimensions={0} | all-to-all | bytes 33792 | tf_op jit(solution)/shard_map/all_to_all | solution.py:253
  207.9 0.7 reshape_reshape_reshape.3
  208.5 0.7 reshape_reshape.3
  (104 shorter events, 5.5 us)
Async XLA Ops:
  0.6 68.8 %copy-start = (bf16[512,2048]{1,0:T(8,128)(2,1)S(1)}, bf16[512,2048]{1,0:T(8,128)(2,1)}, u32[]{:S(2)}) copy-start(bf16[512,2048]{1,0:T(8,128)(2,1)} %param.31) | copy-start | bytes 6291460
  6.7 8.0 %copy-start.10 = (s32[32]{0:T(128)S(1)}, s32[32]{0:T(128)}, u32[]{:S(2)}) copy-start(s32[32]{0:T(128)} %param.23) | copy-start | bytes 388
  8.4 21.7 %all-to-all-start = ((bf16[8,4,4,2048]{3,2,1,0:T(4,128)(2,1)}), bf16[8,4,4,2048]{3,2,1,0:T(4,128)(2,1)S(1)}, u32[]{:S(2)}, u32[]{:S(2)}) async-start(bf16[8,4,4,2048]{3,2,1,0:T(4,128)(2,1)} %fusion.31), calls=%async_computation | async-start | bytes 1048576 | tf_op jit(solution)/shard_map/all_to_all | solution.py:102
  23.6 4.2 %copy-start.6 = (s32[4,32,6]{1,0,2:T(4,128)S(1)}, s32[4,32,6]{1,0,2:T(4,128)}, u32[]{:S(2)}) copy-start(s32[4,32,6]{1,0,2:T(4,128)} %param.25) | copy-start | bytes 9220
  23.6 16.0 %copy-start.7 = (f32[2048]{0:T(1024)S(1)}, f32[2048]{0:T(1024)}, u32[]{:S(2)}) copy-start(f32[2048]{0:T(1024)} %param.27) | copy-start | bytes 24580
  39.7 2.4 %copy-start.3 = (bf16[512,2048]{1,0:T(8,128)(2,1)S(1)}, bf16[512,2048]{1,0:T(8,128)(2,1)}, u32[]{:S(2)}) copy-start(bf16[512,2048]{1,0:T(8,128)(2,1)} %copy.151) | copy-start | bytes 6291460
  39.7 3.2 %copy-start.2 = (bf16[512,2048]{1,0:T(8,128)(2,1)S(1)}, bf16[512,2048]{1,0:T(8,128)(2,1)}, u32[]{:S(2)}) copy-start(bf16[512,2048]{1,0:T(8,128)(2,1)} %copy.152) | copy-start | bytes 6291460
  60.3 4.1 %collective-permute-start = (f32[1,8320]{1,0:T(1,128)S(1)}, f32[1,8320]{1,0:T(1,128)S(1)}, u32[]{:S(2)}, u32[]{:S(2)}) collective-permute-start(f32[1,8320]{1,0:T(1,128)S(1)} %get-tuple-element.18), channel_id=1, source_target_pairs={{0,8},{8,0},{16,24},{24,16},{1,9},{9,1},{17,25},{25,17},{2,10},{10... | collective-permute-start | bytes 99848 | tf_op jit(solution)/shard_map/ppermute | solution.py:166
  60.8 3.9 %collective-permute-start.1 = (f32[1,8320]{1,0:T(1,128)S(1)}, f32[1,8320]{1,0:T(1,128)S(1)}, u32[]{:S(2)}, u32[]{:S(2)}) collective-permute-start(f32[1,8320]{1,0:T(1,128)S(1)} %get-tuple-element.17), channel_id=1, source_target_pairs={{0,16},{8,24},{16,0},{24,8},{1,17},{9,25},{17,1},{25,9},{2,18},{10... | collective-permute-start | bytes 99848 | tf_op jit(solution)/shard_map/ppermute | solution.py:166
  62.4 4.8 %collective-permute-start.2 = (f32[1,8320]{1,0:T(1,128)S(1)}, f32[1,8320]{1,0:T(1,128)S(1)}, u32[]{:S(2)}, u32[]{:S(2)}) collective-permute-start(f32[1,8320]{1,0:T(1,128)S(1)} %get-tuple-element.16), channel_id=1, source_target_pairs={{0,24},{8,16},{16,8},{24,0},{1,25},{9,17},{17,9},{25,1},{2,26},{10... | collective-permute-start | bytes 99848 | tf_op jit(solution)/shard_map/ppermute | solution.py:166
  68.9 10.1 %copy-start.8 = (f32[2048]{0:T(1024)S(1)}, f32[2048]{0:T(1024)}, u32[]{:S(2)}) copy-start(f32[2048]{0:T(1024)} %param.34) | copy-start | bytes 24580
  70.5 32.7 %copy-start.5 = (bf16[2048,64]{0,1:T(8,128)(2,1)S(1)}, bf16[2048,64]{0,1:T(8,128)(2,1)}, u32[]{:S(2)}) copy-start(bf16[2048,64]{0,1:T(8,128)(2,1)} %param.35) | copy-start | bytes 786436
  70.5 8.4 %all-to-all-start.1 = ((f32[4,4,2048]{2,1,0:T(4,128)}), f32[4,4,2048]{2,1,0:T(4,128)S(1)}, u32[]{:S(2)}, u32[]{:S(2)}) async-start(f32[4,4,2048]{2,1,0:T(4,128)} %fusion.9), calls=%async_computation.1 | async-start | bytes 262144 | tf_op jit(solution)/shard_map/all_to_all | solution.py:201
  134.0 1.4 copy-start.4
  139.3 30.7 %copy-start.9 = (f32[2048]{0:T(1024)S(1)}, f32[2048]{0:T(1024)}, u32[]{:S(2)}) copy-start(f32[2048]{0:T(1024)} %param.42) | copy-start | bytes 24580
  193.6 15.6 %copy-start.1 = (bf16[512,2048]{1,0:T(8,128)(2,1)S(1)}, bf16[512,2048]{1,0:T(8,128)(2,1)}, u32[]{:S(2)}) copy-start(bf16[512,2048]{1,0:T(8,128)(2,1)} %param.31) | copy-start | bytes 6291460
